TPU v7x, 512 devices: a whole 4x8x8 slice. The times are simulated.
512 devices in a mesh: seq: 32 (over y, x), head: 16 (over z, core).
Axes of the slice: x: 4, y: 8, z: 8, core: 2. Of those that a mesh axis runs over, the one named last changes fastest.
Arguments:
- features: bfloat16 [65536, 8192], P(('seq', 'head')), may hold values from -6 to 6
- increment_per_head: bfloat16 [65536, 128], P(('seq', 'head')), may hold values from 0.0049743652 to 0.049804688
- token_log_decay: bfloat16 [65536, 128], P(('seq', 'head')), may hold values from -2 to 0, as said below
- b_matrix: bfloat16 [65536, 1024], P(('seq', 'head')), may hold values from -6 to 6
- c_matrix: bfloat16 [65536, 1024], P(('seq', 'head')), may hold values from -0.5 to 0.5
- skip_gain: float32 [128], P('head'), may hold values from 0.5 to 1.5
Outputs:
- mixed_out: bfloat16 [65536, 8192], P(('seq', 'head'))
Inputs may be any that keep to these rules, and one draw needn't show every extreme that they name: `token_log_decay`: log decays are never positive.
All inputs are finite; a program needn't handle non-finite values.
Results may differ from a plain program's by a relative error of at most 0.01.
Values may be sent and summed in bfloat16 or wider, within the bound.
No kernel may reach another device: no remote copies, remote signals or barrier semaphores. Data moves between devices by JAX's collectives and lax.ppermute only.
A program may use at most 128 MiB of HBM per device.

v0:
```python
import jax
import jax.numpy as jnp
from jax import lax
from jax.sharding import PartitionSpec as P

G = 8
Q = 128


def prefix_2(value, axis, combine, identity):
    size, index = (lax.axis_size(axis), lax.axis_index(axis))
    everything = jax.tree.map(
        lambda part, kind: lax.all_gather(part.astype(kind), axis),
        value,
        (jnp.bfloat16, jnp.bfloat16),
    )
    start = jax.tree.map(
        lambda part, zero: jnp.broadcast_to(jnp.asarray(zero, part.dtype), part.shape),
        value,
        identity,
    )

    def lap(k, before):
        reached = k < index
        new = combine(
            before, jax.tree.map(lambda part, own: part[k].astype(own.dtype), everything, value)
        )
        return jax.tree.map(lambda a, b: jnp.where(reached, a, b), new, before)

    return lax.fori_loop(0, size, lap, start)


def combine(earlier, latter):
    return (earlier[0] + latter[0], jnp.exp(latter[0])[:, None, None] * earlier[1] + latter[1])


def local(features, increment_per_head, token_log_decay, b_matrix, c_matrix, skip_gain):
    n_groups = lax.axis_size("head")
    local_rows = features.shape[0]
    head_count = increment_per_head.shape[1]
    local_heads = head_count // n_groups
    head_width = features.shape[1] // head_count
    state_width = b_matrix.shape[1] // G
    b_slots = jnp.repeat(b_matrix.reshape(local_rows, G, state_width), n_groups // G, axis=1)
    c_slots = jnp.repeat(c_matrix.reshape(local_rows, G, state_width), n_groups // G, axis=1)
    local_groups = max(1, G // n_groups)
    per_group = local_heads // local_groups
    paired = jnp.concatenate([b_slots, c_slots], axis=2)
    rates = jnp.concatenate(
        [
            increment_per_head.reshape(local_rows, n_groups, local_heads),
            token_log_decay.reshape(local_rows, n_groups, local_heads),
        ],
        axis=2,
    )
    blocks_in = features.reshape(local_rows, n_groups, local_heads * head_width)
    moved_x, moved_rates, moved_bc = (
        lax.all_to_all(blocks_in, "head", split_axis=1, concat_axis=0, tiled=True),
        lax.all_to_all(rates, "head", split_axis=1, concat_axis=0, tiled=True),
        lax.all_to_all(paired, "head", split_axis=1, concat_axis=0, tiled=True),
    )
    token_count = local_rows * n_groups
    block_count = token_count // Q
    grouped_input_matrix = moved_x.reshape(block_count, Q, local_heads, head_width)
    step_local = (
        moved_rates[:, 0, :local_heads]
        .astype(jnp.float32)
        .reshape(block_count, Q, local_heads)
        .transpose(0, 2, 1)
    )
    shrinkage_within_segment = (
        moved_rates[:, 0, local_heads:]
        .astype(jnp.float32)
        .reshape(block_count, Q, local_heads)
        .transpose(0, 2, 1)
    )
    b_local = moved_bc[:, 0, : local_groups * state_width].reshape(
        block_count, Q, local_groups, state_width
    )
    c_local = moved_bc[:, 0, local_groups * state_width :].reshape(
        block_count, Q, local_groups, state_width
    )
    within = jnp.cumsum(shrinkage_within_segment, axis=2)
    block_total = within[:, :, -1]
    scores = jnp.einsum("ctgn,csgn->cgts", c_local, b_local, preferred_element_type=jnp.float32)
    scores = jnp.repeat(scores, per_group, axis=1)
    causal = (jnp.arange(Q)[:, None] >= jnp.arange(Q)[None, :])[None, None]
    gap_log = within[:, :, :, None] - within[:, :, None, :]
    damping = jnp.where(causal, jnp.exp(jnp.where(causal, gap_log, 0.0)), 0.0)
    weight = (scores * damping * step_local[:, :, None, :]).astype(jnp.bfloat16)
    inside = jnp.einsum(
        "chts,cshp->cthp", weight, grouped_input_matrix, preferred_element_type=jnp.float32
    )
    factor = (jnp.exp(block_total[:, :, None] - within) * step_local).transpose(0, 2, 1)
    scaled = (grouped_input_matrix * factor[..., None]).astype(jnp.bfloat16)
    update = jnp.einsum(
        "csgn,csgkp->cgknp",
        b_local,
        scaled.reshape(block_count, Q, local_groups, per_group, head_width),
        preferred_element_type=jnp.float32,
    ).reshape(block_count, local_heads, state_width, head_width)

    def advance(state_now, inputs):
        total_now, update_now = inputs
        return (jnp.exp(total_now)[:, None, None] * state_now + update_now, state_now)

    dev_state, local_carried = lax.scan(
        advance,
        jnp.zeros((local_heads, state_width, head_width), jnp.float32),
        (block_total, update),
    )
    prefix = jnp.cumsum(block_total, axis=0) - block_total
    dev_total = jnp.sum(block_total, axis=0)
    _, incoming = prefix_2(
        (dev_total, dev_state),
        "seq",
        combine,
        (jnp.zeros_like(dev_total), jnp.zeros_like(dev_state)),
    )
    carried = local_carried + jnp.exp(prefix)[:, :, None, None] * incoming[None]
    carried_in = carried.astype(jnp.bfloat16)
    outside = jnp.einsum(
        "ctgn,cgknp->ctgkp",
        c_local,
        carried_in.reshape(block_count, local_groups, per_group, state_width, head_width),
        preferred_element_type=jnp.float32,
    ).reshape(block_count, Q, local_heads, head_width)
    mixed = (
        inside
        + jnp.exp(within).transpose(0, 2, 1)[..., None] * outside
        + skip_gain[None, None, :, None] * grouped_input_matrix
    )
    leaving = mixed.astype(jnp.bfloat16).reshape(token_count, 1, local_heads * head_width)
    returned = lax.all_to_all(leaving, "head", split_axis=0, concat_axis=1, tiled=True)
    return returned.reshape(local_rows, head_count * head_width)


def solution(mesh):
    in_specs = (
        P(("seq", "head"), None),
        P(("seq", "head"), None),
        P(("seq", "head"), None),
        P(("seq", "head"), None),
        P(("seq", "head"), None),
        P("head"),
    )
    out_specs = P(("seq", "head"), None)
    return jax.shard_map(local, mesh=mesh, in_specs=in_specs, out_specs=out_specs, check_vma=False)
```

profile of v0, /device:TPU:1, one launch (start us, length us, event | category | flops | bytes accessed | tf_op | source)
XLA Modules:
  0.0 408.8 jit_solution(9127890750724101850)
XLA Ops:
  6.5 1.0 copy.52
  9.1 11.8 %all-to-all-start.1 = ((bf16[128,16,16]{0,2,1:T(8,128)(2,1)}), bf16[128,16,16]{0,2,1:T(8,128)(2,1)S(1)}, u32[]{:S(2)}, u32[]{:S(2)}) async-start(bf16[128,16,16]{0,2,1:T(8,128)(2,1)} %pad_maximum_fusion.1), calls=%async_computation.1 | async-start | bytes 131072 | tf_op jit(solution)/shard_map/all_to_all | solution.py:59
  21.0 1.0 copy_bitcast_fusion.1
  22.2 1.1 pad_maximum_fusion
  23.3 5.4 %all-to-all-done.1 = bf16[128,16,16]{0,2,1:T(8,128)(2,1)S(1)} async-done(((bf16[128,16,16]{0,2,1:T(8,128)(2,1)}), bf16[128,16,16]{0,2,1:T(8,128)(2,1)S(1)}, u32[]{:S(2)}, u32[]{:S(2)}) %all-to-all-start.1) | async-done | bytes 65568 | tf_op jit(solution)/shard_map/all_to_all | solution.py:59
  28.7 3.6 all-to-all-start
  32.3 2.4 copy.71
  34.8 25.5 %all-to-all-done = bf16[128,16,256]{2,0,1:T(8,128)(2,1)S(1)} async-done(((bf16[128,16,256]{2,0,1:T(8,128)(2,1)}), bf16[128,16,256]{2,0,1:T(8,128)(2,1)S(1)}, u32[]{:S(2)}, u32[]{:S(2)}) %all-to-all-start) | async-done | bytes 1048608 | tf_op jit(solution)/shard_map/all_to_all | solution.py:60
  60.3 1.0 copy-done.3
  61.4 3.6 all-to-all-start.2
  65.7 4.5 %reduce_window_sum.22 = f32[16,8,128]{2,1,0:T(8,128)S(1)} reduce-window(f32[16,8,128]{2,1,0:T(8,128)S(1)} %get-tuple-element.214, f32[]{:T(128)} %constant.47.clone.1), window={size=1x1x128 pad=0_0x0_0x127_0}, to_apply=%region_0.0 | reduce-window | flops 2080768 | bytes 131076 | tf_op jit(solution)/shard_map/jit(cumsum)/reduce_window_sum | solution.py:83
  70.7 2.1 fusion.20
  72.7 41.1 %all-to-all-done.2 = bf16[128,16,512]{0,2,1:T(8,128)(2,1)S(1)} async-done(((bf16[128,16,512]{0,2,1:T(8,128)(2,1)}), bf16[128,16,512]{0,2,1:T(8,128)(2,1)S(1)}, u32[]{:S(2)}, u32[]{:S(2)}) %all-to-all-start.2) | async-done | bytes 2097184 | tf_op jit(solution)/shard_map/all_to_all | solution.py:58
  113.8 4.1 convolution_bitcast_fusion
  117.9 34.9 %while.27 = (s32[]{:T(128)}, f32[8,128,64]{2,1,0:T(8,128)S(1)}, f32[16,8,128,64]{3,2,1,0:T(8,128)}, f32[16,8]{1,0:T(8,128)S(1)}, f32[16,8,128,64]{2,3,1,0:T(8,128)}, /*index=5*/s32[]{:T(128)}, s32[]{:T(128)}) while((s32[]{:T(128)}, f32[8,128,64]{2,1,0:T(8,128)S(1)}, f32[16,8,128,64]{3,2,1,0:T(8,128)}, f32[16,8]{1,0:T(8,128)S(1)}, ...), condition=%wide.region_2.3_spmd.clone, body=%wide.region_1.2_spmd.clone.sunk | while | flops 262147 | bytes 2621644 | solution.py:107
  118.7 1.0 constant_dynamic-slice_fusion.5
  120.9 1.0 constant_dynamic-slice_fusion.5
  123.1 1.0 constant_dynamic-slice_fusion.5
  125.3 1.0 constant_dynamic-slice_fusion.5
  127.4 1.0 constant_dynamic-slice_fusion.5
  129.6 1.0 constant_dynamic-slice_fusion.5
  131.8 1.0 constant_dynamic-slice_fusion.5
  134.0 1.0 constant_dynamic-slice_fusion.5
  136.1 1.0 constant_dynamic-slice_fusion.5
  138.3 1.0 constant_dynamic-slice_fusion.5
  140.5 1.0 constant_dynamic-slice_fusion.5
  142.7 1.0 constant_dynamic-slice_fusion.5
  144.9 1.0 constant_dynamic-slice_fusion.5
  147.1 1.0 constant_dynamic-slice_fusion.5
  149.2 1.0 constant_dynamic-slice_fusion.5
  151.4 1.0 constant_dynamic-slice_fusion.5
  153.6 1.3 dynamic-slice
  155.8 61.7 %all-reduce = bf16[256]{0:T(256)(128)(2,1)S(1)} all-reduce(bf16[256]{0:T(256)(128)(2,1)S(1)} %dynamic-update-slice), channel_id=2, replica_groups=mesh['seq'=32,'head'=16] {'seq'}, use_global_device_ids=true, to_apply=%add | all-reduce | flops 256 | bytes 1024
  217.6 2.6 fusion.21
  220.2 16.5 %all-gather.4.cloned.1.call-done = bf16[256,128,64]{1,2,0:T(8,128)(2,1)} async-done(((bf16[8,128,64]{1,2,0:T(8,128)(2,1)}), bf16[256,128,64]{1,2,0:T(8,128)(2,1)}) %all-gather.4.cloned.1.call-update) | async-done | bytes 4194320 | tf_op jit(solution)/shard_map/all_gather | solution.py:13
  236.7 41.5 %while.28 = (s32[]{:T(128)}, f32[8,128,64]{2,1,0:T(8,128)S(1)}, s32[]{:T(128)}, bf16[32,8]{1,0:T(8,128)(2,1)S(1)}, bf16[32,8,128,64]{2,3,1,0:T(8,128)(2,1)}, /*index=5*/s32[]{:T(128)}, s32[]{:T(128)}) while((s32[]{:T(128)}, f32[8,128,64]{2,1,0:T(8,128)S(1)}, s32[]{:T(128)}, bf16[32,8]{1,0:T(8,128)(2,1)S(1)}, ...), condition=%wide.region_6.7_spmd.clone, body=%wide.region_5.6_spmd.clone.sunk | while | flops 327692 | bytes 1179841 | solution.py:30
  239.3 0.9 constant_dynamic-slice_fusion.6
  278.3 6.0 %fusion.7 = f32[16,8,64,128]{3,2,1,0:T(8,128)S(1)} fusion(bf16[16,128,128,1]{2,1,3,0:T(8,128)(2,1)S(1)} %bitcast.127, f32[16,8,128,64]{3,2,1,0:T(8,128)} %get-tuple-element.127, f32[8,128,64]{2,1,0:T(8,128)S(1)} %get-tuple-element.129, f32[16,8]{1,0:T(8,128)S(1)} %subtract_exponential_fusion), kind=kOutput, calls=%fused_computation.18 | convolution fusion | flops 271581184 | bytes 9175552 | tf_op jit(solution)/shard_map/ctgn,cgknp->ctgkp/dot_general | solution.py:122
  284.3 4.2 %fusion.6 = bf16[16,128,8,64]{1,3,2,0:T(8,128)(2,1)S(1)} fusion(bf16[16,128,8,64]{1,3,2,0:T(8,128)(2,1)S(1)} %bitcast.123, f32[16,8,64,128]{3,2,1,0:T(8,128)S(1)} %fusion.7, f32[8]{0:T(128)S(1)} %copy-done.7, f32[16,128,8]{1,2,0:T(8,128)S(1)} %exponential_bitcast_fusion.1, f32[16,8,128]{2,1,0:T(8,128)S(1)} %copy-done.6, ...), kind=kOutput, calls=%fused_computation.17 | convolution fusion | flops 287309824 | bytes 9650208 | tf_op jit(solution)/shard_map/chts,cshp->cthp/dot_general | solution.py:91
  288.5 3.6 copy.76
  292.1 14.9 %reshape.157 = bf16[2048,1,512]{2,1,0:T(2,128)(2,1)} reshape(bf16[16,128,8,64]{3,2,1,0:T(8,128)(2,1)} %copy.76) | data formatting | bytes 4194304 | tf_op jit(solution)/shard_map/reshape | solution.py:133
  307.5 14.1 %reduce.1 = bf16[2048,512]{1,0:T(8,128)(2,1)S(1)} reduce(bf16[2048,1,512]{2,1,0:T(2,128)(2,1)} %reshape.157, bf16[]{:T(256)} %broadcast.37), dimensions={1}, to_apply=%reshape.157.reduce_sub_computation | reduce | bytes 4194306 | tf_op jit(solution)/shard_map/reshape | solution.py:133
  321.6 2.8 reshape.164
  324.3 61.7 %all_to_all.66 = bf16[16,2,32768]{2,1,0:T(2,128)(2,1)S(1)} all-to-all(bf16[16,2,32768]{2,1,0:T(2,128)(2,1)} %reshape.164), channel_id=1, replica_groups=mesh['seq'=32,'head'=16] {'head'}, dimensions={0} | all-to-all | bytes 4194304 | tf_op jit(solution)/shard_map/all_to_all | solution.py:134
  386.1 6.7 %reshape.165 = bf16[2048,1,512]{2,1,0:T(2,128)(2,1)} reshape(bf16[16,2,32768]{2,1,0:T(2,128)(2,1)S(1)} %all_to_all.66) | data formatting | bytes 4194304
  392.7 2.8 copy.80
  395.5 2.4 copy.66
  397.9 4.1 copy.67
  (230 shorter events, 62.6 us)
Async XLA Ops:
  6.5 14.4 %copy-start = (bf16[128,1024]{1,0:T(8,128)(2,1)S(1)}, bf16[128,1024]{1,0:T(8,128)(2,1)}, u32[]{:S(2)}) copy-start(bf16[128,1024]{1,0:T(8,128)(2,1)} %param.14) | copy-start | bytes 786436
  6.5 25.8 %copy-start.4 = (bf16[128,8192]{1,0:T(8,128)(2,1)S(1)}, bf16[128,8192]{1,0:T(8,128)(2,1)}, u32[]{:S(2)}) copy-start(bf16[128,8192]{1,0:T(8,128)(2,1)} %param.10) | copy-start | bytes 6291460
  9.1 19.6 %all-to-all-start.1 = ((bf16[128,16,16]{0,2,1:T(8,128)(2,1)}), bf16[128,16,16]{0,2,1:T(8,128)(2,1)S(1)}, u32[]{:S(2)}, u32[]{:S(2)}) async-start(bf16[128,16,16]{0,2,1:T(8,128)(2,1)} %pad_maximum_fusion.1), calls=%async_computation.1 | async-start | bytes 131072 | tf_op jit(solution)/shard_map/all_to_all | solution.py:59
  28.7 31.6 %all-to-all-start = ((bf16[128,16,256]{2,0,1:T(8,128)(2,1)}), bf16[128,16,256]{2,0,1:T(8,128)(2,1)S(1)}, u32[]{:S(2)}, u32[]{:S(2)}) async-start(bf16[128,16,256]{2,0,1:T(8,128)(2,1)} %pad_maximum_fusion), calls=%async_computation | async-start | bytes 2097152 | tf_op jit(solution)/shard_map/all_to_all | solution.py:60
  60.3 1.0 copy-start.3
  61.4 52.5 %all-to-all-start.2 = ((bf16[128,16,512]{0,2,1:T(8,128)(2,1)}), bf16[128,16,512]{0,2,1:T(8,128)(2,1)S(1)}, u32[]{:S(2)}, u32[]{:S(2)}) async-start(bf16[128,16,512]{0,2,1:T(8,128)(2,1)} %bitcast.124), calls=%async_computation.2 | async-start | bytes 4194304 | tf_op jit(solution)/shard_map/all_to_all | solution.py:58
  65.0 171.8 %all-gather.4.cloned.1.call-start = ((), (), s32[]{:S(2)}) async-start(), calls=%async_computation.4 | async-start | bytes 4325376 | tf_op jit(solution)/shard_map/all_gather | solution.py:13
  113.8 4.1 copy-start.1
  278.2 6.0 %copy-start.2 = (bf16[128,16,512]{0,2,1:T(8,128)(2,1)S(1)}, bf16[128,16,512]{0,2,1:T(8,128)(2,1)}, u32[]{:S(2)}) copy-start(bf16[128,16,512]{0,2,1:T(8,128)(2,1)} %copy-done.1) | copy-start | bytes 6291460
  278.2 6.0 %copy-start.5 = (f32[16,128,128]{2,1,0:T(8,128)S(1)}, f32[16,128,128]{2,1,0:T(8,128)}, u32[]{:S(2)}) copy-start(f32[16,128,128]{2,1,0:T(8,128)} %fusion.21) | copy-start | bytes 3145732
  278.2 6.0 %copy-start.6 = (f32[16,8,128]{2,1,0:T(8,128)S(1)}, f32[16,8,128]{2,1,0:T(8,128)}, u32[]{:S(2)}) copy-start(f32[16,8,128]{2,1,0:T(8,128)} %get-tuple-element.213) | copy-start | bytes 196612
  278.2 6.0 %copy-start.7 = (f32[8]{0:T(128)S(1)}, f32[8]{0:T(128)}, u32[]{:S(2)}) copy-start(f32[8]{0:T(128)} %param.15) | copy-start | bytes 100
Sparse Core Ops, SparseCore 0:
  153.7 83.0 all-gather.3
where the time goes:
time: 411 us; the launch traced here: 409 us
  blocking collectives  123 us (30%)
  local copies, waits for them, and re-layouts  103 us (25%)
  waiting for transfers between devices  88.6 us (22%)
  other arithmetic  41.7 us (10%)
  starting transfers between devices  19.1 us (5%)
  matrix products  16.8 us (4%)
  between operations  14.3 us (3%)
    all_to_all x1, blocking collectives, local(): lax.all_to_all(leaving, 'head', split_axis=0, concat_axis=1, tiled=True)  61.7 us
    unnamed x1, blocking collectives  61.7 us
    all_to_all x1, waiting for transfers between devices, local(): lax.all_to_all(blocks_in, 'head', split_axis=1, concat_axis=0, tiled=True)  41.1 us
    dynamic_slice x64, local copies, waits for them, and re-layouts, lap(): part[k].astype(own.dtype)  35.1 us
    all_to_all x1, waiting for transfers between devices, local(): lax.all_to_all(paired, 'head', split_axis=1, concat_axis=0, tiled=True)  25.5 us
    reshape x3, local copies, waits for them, and re-layouts, local(): mixed.astype(jnp.bfloat16).reshape(token_count, 1, local_heads * head_width)  19 us
    dynamic_slice x32, local copies, waits for them, and re-layouts, local(): lax.scan(advance, jnp.zeros((local_heads, state_width, head_width), jnp.f...  18.7 us
    unnamed x24, local copies, waits for them, and re-layouts  16.7 us
  transfers between devices with their start and end apart: 4, of which 4 were waited for; matrix products, arithmetic and copies ran while one was open for 4% of the time, Pallas kernels for 0%

commit v1 on v0

--- a/solution.py
+++ b/solution.py
@@ -131,7 +131,10 @@
         + skip_gain[None, None, :, None] * grouped_input_matrix
     )
     leaving = mixed.astype(jnp.bfloat16).reshape(token_count, 1, local_heads * head_width)
-    returned = lax.all_to_all(leaving, "head", split_axis=0, concat_axis=1, tiled=True)
+    returned = jnp.concatenate(
+        lax.all_to_all(jnp.stack(jnp.split(leaving, lax.axis_size("head"), axis=0)), "head", 0, 0),
+        axis=1,
+    )
     return returned.reshape(local_rows, head_count * head_width)
 
 

time: 411 us -> 362 us (0.88)
  local copies, waits for them, and re-layouts: 103 us -> 68.6 us
  other arithmetic: 41.7 us -> 27.8 us
    reshape x4 -> x0, local copies, waits for them, and re-layouts: 23.1 us -> none  [the longest x3 19 us: local(): mixed.astype(jnp.bfloat16).reshape(token_count, 1, local_heads * head_width)]
    reshape x1 -> x0, other arithmetic: 14.1 us -> none  [local(): mixed.astype(jnp.bfloat16).reshape(token_count, 1, local_heads * head_width)]
    unnamed x24 -> x38, local copies, waits for them, and re-layouts: 16.7 us -> 4.68 us
where the time goes in v1:
time: 362 us; the launch traced here: 360 us
  blocking collectives  123 us (34%)
  waiting for transfers between devices  89.7 us (25%)
  local copies, waits for them, and re-layouts  68.6 us (19%)
  other arithmetic  27.8 us (8%)
  starting transfers between devices  19.1 us (5%)
  matrix products  15.8 us (4%)
  between operations  14.4 us (4%)
    unnamed x1, blocking collectives  61.7 us
    all_to_all x1, blocking collectives, local(): lax.all_to_all(jnp.stack(jnp.split(leaving, lax.axis_size('head'), axis=0...  61.5 us
    all_to_all x1, waiting for transfers between devices, local(): lax.all_to_all(blocks_in, 'head', split_axis=1, concat_axis=0, tiled=True)  41.1 us
    dynamic_slice x64, local copies, waits for them, and re-layouts, lap(): part[k].astype(own.dtype)  35.1 us
    all_to_all x1, waiting for transfers between devices, local(): lax.all_to_all(paired, 'head', split_axis=1, concat_axis=0, tiled=True)  25.5 us
    dynamic_slice x32, local copies, waits for them, and re-layouts, local(): lax.scan(advance, jnp.zeros((local_heads, state_width, head_width), jnp.f...  18.7 us
    all_gather x1, waiting for transfers between devices, prefix_2(): lax.all_gather(part.astype(kind), axis)  17.7 us
    dynamic_update_slice x16, other arithmetic, local(): lax.scan(advance, jnp.zeros((local_heads, state_width, head_width), jnp.f...  13.6 us
  transfers between devices with their start and end apart: 4, of which 4 were waited for; matrix products, arithmetic and copies ran while one was open for 4% of the time, Pallas kernels for 0%

profile of v1, /device:TPU:1, one launch (start us, length us, event | category | flops | bytes accessed | tf_op | source)
XLA Modules:
  0.0 360.4 jit_solution(12915998516612345840)
XLA Ops:
  9.0 11.8 %all-to-all-start.1 = ((bf16[128,16,16]{0,2,1:T(8,128)(2,1)}), bf16[128,16,16]{0,2,1:T(8,128)(2,1)S(1)}, u32[]{:S(2)}, u32[]{:S(2)}) async-start(bf16[128,16,16]{0,2,1:T(8,128)(2,1)} %pad_maximum_fusion.1), calls=%async_computation.1 | async-start | bytes 131072 | tf_op jit(solution)/shard_map/all_to_all | solution.py:59
  20.9 1.0 copy_bitcast_fusion.1
  22.1 1.1 pad_maximum_fusion
  23.2 5.4 %all-to-all-done.1 = bf16[128,16,16]{0,2,1:T(8,128)(2,1)S(1)} async-done(((bf16[128,16,16]{0,2,1:T(8,128)(2,1)}), bf16[128,16,16]{0,2,1:T(8,128)(2,1)S(1)}, u32[]{:S(2)}, u32[]{:S(2)}) %all-to-all-start.1) | async-done | bytes 65568 | tf_op jit(solution)/shard_map/all_to_all | solution.py:59
  28.6 3.6 all-to-all-start
  32.2 2.4 copy.51
  34.7 25.5 %all-to-all-done = bf16[128,16,256]{2,0,1:T(8,128)(2,1)S(1)} async-done(((bf16[128,16,256]{2,0,1:T(8,128)(2,1)}), bf16[128,16,256]{2,0,1:T(8,128)(2,1)S(1)}, u32[]{:S(2)}, u32[]{:S(2)}) %all-to-all-start) | async-done | bytes 1048608 | tf_op jit(solution)/shard_map/all_to_all | solution.py:60
  60.2 1.1 copy-done.4
  61.3 3.6 %all-to-all-start.2 = ((bf16[128,16,512]{0,2,1:T(8,128)(2,1)}), bf16[128,16,512]{0,2,1:T(8,128)(2,1)S(1)}, u32[]{:S(2)}, u32[]{:S(2)}) async-start(bf16[128,16,512]{0,2,1:T(8,128)(2,1)} %bitcast.168), calls=%async_computation.2 | async-start | bytes 4194304 | tf_op jit(solution)/shard_map/all_to_all | solution.py:58
  65.6 4.5 %reduce_window_sum.22 = f32[16,8,128]{2,1,0:T(8,128)S(1)} reduce-window(f32[16,8,128]{2,1,0:T(8,128)S(1)} %get-tuple-element.225, f32[]{:T(128)} %constant.47.clone.1), window={size=1x1x128 pad=0_0x0_0x127_0}, to_apply=%region_0.0 | reduce-window | flops 2080768 | bytes 131076 | tf_op jit(solution)/shard_map/jit(cumsum)/reduce_window_sum | solution.py:83
  70.6 2.1 fusion.21
  72.7 41.1 %all-to-all-done.2 = bf16[128,16,512]{0,2,1:T(8,128)(2,1)S(1)} async-done(((bf16[128,16,512]{0,2,1:T(8,128)(2,1)}), bf16[128,16,512]{0,2,1:T(8,128)(2,1)S(1)}, u32[]{:S(2)}, u32[]{:S(2)}) %all-to-all-start.2) | async-done | bytes 2097184 | tf_op jit(solution)/shard_map/all_to_all | solution.py:58
  113.7 4.1 %convolution_bitcast_fusion = f32[16,8,128,64]{2,3,1,0:T(8,128)} fusion(bf16[16,128,128,1]{2,1,3,0:T(8,128)(2,1)} %bitcast.172, bf16[16,128,8,64]{1,3,2,0:T(8,128)(2,1)S(1)} %bitcast.166, f32[16,128,8]{1,2,0:T(8,128)S(1)} %convert_multiply_fusion.2), kind=kOutput, calls=%fused_computation.29 | convolution fusion | flops 271581184 | bytes 6881280 | tf_op jit(solution)/shard_map/csgn,csgkp->cgknp/dot_general | solution.py:96
  117.8 35.0 %while.27 = (s32[]{:T(128)}, f32[8,128,64]{2,1,0:T(8,128)S(1)}, f32[16,8,128,64]{3,2,1,0:T(8,128)}, f32[16,8]{1,0:T(8,128)S(1)}, f32[16,8,128,64]{2,3,1,0:T(8,128)}, /*index=5*/s32[]{:T(128)}, s32[]{:T(128)}) while((s32[]{:T(128)}, f32[8,128,64]{2,1,0:T(8,128)S(1)}, f32[16,8,128,64]{3,2,1,0:T(8,128)}, f32[16,8]{1,0:T(8,128)S(1)}, ...), condition=%wide.region_2.3_spmd.clone, body=%wide.region_1.2_spmd.clone.sunk | while | flops 262147 | bytes 2621644 | solution.py:107
  118.6 1.0 constant_dynamic-slice_fusion.5
  120.8 1.0 constant_dynamic-slice_fusion.5
  123.0 1.0 constant_dynamic-slice_fusion.5
  125.2 1.0 constant_dynamic-slice_fusion.5
  127.4 1.0 constant_dynamic-slice_fusion.5
  129.6 1.0 constant_dynamic-slice_fusion.5
  131.8 1.0 constant_dynamic-slice_fusion.5
  134.0 1.0 constant_dynamic-slice_fusion.5
  136.1 1.0 constant_dynamic-slice_fusion.5
  138.3 1.0 constant_dynamic-slice_fusion.5
  140.5 1.0 constant_dynamic-slice_fusion.5
  142.7 1.0 constant_dynamic-slice_fusion.5
  144.9 1.0 constant_dynamic-slice_fusion.5
  147.1 1.0 constant_dynamic-slice_fusion.5
  149.2 1.0 constant_dynamic-slice_fusion.5
  151.5 1.0 constant_dynamic-slice_fusion.5
  153.6 1.3 dynamic-slice
  155.8 61.7 %all-reduce = bf16[256]{0:T(256)(128)(2,1)S(1)} all-reduce(bf16[256]{0:T(256)(128)(2,1)S(1)} %dynamic-update-slice), channel_id=2, replica_groups=mesh['seq'=32,'head'=16] {'seq'}, use_global_device_ids=true, to_apply=%add | all-reduce | flops 256 | bytes 1024
  217.6 1.5 fusion.22
  219.1 17.7 %all-gather.4.cloned.1.call-done = bf16[256,128,64]{1,2,0:T(8,128)(2,1)} async-done(((bf16[8,128,64]{1,2,0:T(8,128)(2,1)}), bf16[256,128,64]{1,2,0:T(8,128)(2,1)}) %all-gather.4.cloned.1.call-update) | async-done | bytes 4194320 | tf_op jit(solution)/shard_map/all_gather | solution.py:13
  236.8 41.5 %while.28 = (s32[]{:T(128)}, f32[8,128,64]{2,1,0:T(8,128)S(1)}, s32[]{:T(128)}, bf16[32,8]{1,0:T(8,128)(2,1)S(1)}, bf16[32,8,128,64]{2,3,1,0:T(8,128)(2,1)}, /*index=5*/s32[]{:T(128)}, s32[]{:T(128)}) while((s32[]{:T(128)}, f32[8,128,64]{2,1,0:T(8,128)S(1)}, s32[]{:T(128)}, bf16[32,8]{1,0:T(8,128)(2,1)S(1)}, ...), condition=%wide.region_6.7_spmd.clone, body=%wide.region_5.6_spmd.clone.sunk | while | flops 327692 | bytes 1179841 | solution.py:30
  242.0 0.9 constant_dynamic-slice_fusion.6
  243.3 0.9 constant_dynamic-slice_fusion.6
  248.5 0.9 constant_dynamic-slice_fusion.6
  249.8 0.9 constant_dynamic-slice_fusion.6
  253.7 0.9 constant_dynamic-slice_fusion.6
  255.0 0.9 constant_dynamic-slice_fusion.6
  260.1 0.9 constant_dynamic-slice_fusion.6
  261.4 0.9 constant_dynamic-slice_fusion.6
  266.6 0.9 constant_dynamic-slice_fusion.6
  278.3 6.0 %fusion.7 = f32[16,8,64,128]{3,2,1,0:T(8,128)S(1)} fusion(bf16[16,128,128,1]{2,1,3,0:T(8,128)(2,1)S(1)} %bitcast.171, f32[16,8,128,64]{3,2,1,0:T(8,128)} %get-tuple-element.127, f32[8,128,64]{2,1,0:T(8,128)S(1)} %get-tuple-element.129, f32[16,8]{1,0:T(8,128)S(1)} %subtract_exponential_fusion), kind=kOutput, calls=%fused_computation.18 | convolution fusion | flops 271581184 | bytes 9175552 | tf_op jit(solution)/shard_map/ctgn,cgknp->ctgkp/dot_general | solution.py:122
  284.4 4.2 %fusion.6 = bf16[16,128,8,64]{1,3,2,0:T(8,128)(2,1)S(1)} fusion(bf16[16,128,8,64]{1,3,2,0:T(8,128)(2,1)S(1)} %bitcast.167, f32[16,8,64,128]{3,2,1,0:T(8,128)S(1)} %fusion.7, f32[8]{0:T(128)S(1)} %copy-done.8, f32[16,128,8]{1,2,0:T(8,128)S(1)} %exponential_bitcast_fusion.1, f32[16,8,128]{2,1,0:T(8,128)S(1)} %copy-done.7, ...), kind=kOutput, calls=%fused_computation.17 | convolution fusion | flops 287309824 | bytes 9650208 | tf_op jit(solution)/shard_map/chts,cshp->cthp/dot_general | solution.py:91
  289.2 61.5 %all_to_all.56 = bf16[16,128,1,512]{1,3,2,0:T(8,128)(2,1)S(1)} all-to-all(bf16[16,128,1,512]{1,3,2,0:T(8,128)(2,1)S(1)} %bitcast_dynamic-update-slice_fusion.1), channel_id=1, replica_groups=mesh['seq'=32,'head'=16] {'head'}, dimensions={0} | all-to-all | bytes 4194304 | tf_op jit(solution)/shard_map/all_to_all | solution.py:135
  350.7 2.9 copy.56
  (241 shorter events, 56.3 us)
Async XLA Ops:
  6.5 14.3 %copy-start = (bf16[128,1024]{1,0:T(8,128)(2,1)S(1)}, bf16[128,1024]{1,0:T(8,128)(2,1)}, u32[]{:S(2)}) copy-start(bf16[128,1024]{1,0:T(8,128)(2,1)} %param.14) | copy-start | bytes 786436
  9.0 19.6 %all-to-all-start.1 = ((bf16[128,16,16]{0,2,1:T(8,128)(2,1)}), bf16[128,16,16]{0,2,1:T(8,128)(2,1)S(1)}, u32[]{:S(2)}, u32[]{:S(2)}) async-start(bf16[128,16,16]{0,2,1:T(8,128)(2,1)} %pad_maximum_fusion.1), calls=%async_computation.1 | async-start | bytes 131072 | tf_op jit(solution)/shard_map/all_to_all | solution.py:59
  22.1 10.1 %copy-start.5 = (bf16[128,8192]{1,0:T(8,128)(2,1)S(1)}, bf16[128,8192]{1,0:T(8,128)(2,1)}, u32[]{:S(2)}) copy-start(bf16[128,8192]{1,0:T(8,128)(2,1)} %param.10) | copy-start | bytes 6291460
  28.6 31.6 %all-to-all-start = ((bf16[128,16,256]{2,0,1:T(8,128)(2,1)}), bf16[128,16,256]{2,0,1:T(8,128)(2,1)S(1)}, u32[]{:S(2)}, u32[]{:S(2)}) async-start(bf16[128,16,256]{2,0,1:T(8,128)(2,1)} %pad_maximum_fusion), calls=%async_computation | async-start | bytes 2097152 | tf_op jit(solution)/shard_map/all_to_all | solution.py:60
  60.2 1.1 copy-start.4
  61.3 52.5 %all-to-all-start.2 = ((bf16[128,16,512]{0,2,1:T(8,128)(2,1)}), bf16[128,16,512]{0,2,1:T(8,128)(2,1)S(1)}, u32[]{:S(2)}, u32[]{:S(2)}) async-start(bf16[128,16,512]{0,2,1:T(8,128)(2,1)} %bitcast.168), calls=%async_computation.2 | async-start | bytes 4194304 | tf_op jit(solution)/shard_map/all_to_all | solution.py:58
  64.9 171.9 %all-gather.4.cloned.1.call-start = ((), (), s32[]{:S(2)}) async-start(), calls=%async_computation.4 | async-start | bytes 4325376 | tf_op jit(solution)/shard_map/all_gather | solution.py:13
  113.7 4.1 %copy-start.1 = (bf16[128,16,512]{0,2,1:T(8,128)(2,1)}, bf16[128,16,512]{0,2,1:T(8,128)(2,1)S(1)}, u32[]{:S(2)}) copy-start(bf16[128,16,512]{0,2,1:T(8,128)(2,1)S(1)} %all-to-all-done.2) | copy-start | bytes 6291460
  117.8 99.8 %copy-start.3 = (bf16[2048,1,128]{2,0,1:T(8,128)(2,1)S(1)}, bf16[2048,1,128]{2,0,1:T(8,128)(2,1)}, u32[]{:S(2)}) copy-start(bf16[2048,1,128]{2,0,1:T(8,128)(2,1)} %get-tuple-element.222) | copy-start | bytes 1572868
  278.3 6.0 %copy-start.2 = (bf16[128,16,512]{0,2,1:T(8,128)(2,1)S(1)}, bf16[128,16,512]{0,2,1:T(8,128)(2,1)}, u32[]{:S(2)}) copy-start(bf16[128,16,512]{0,2,1:T(8,128)(2,1)} %copy-done.1) | copy-start | bytes 6291460
  278.3 6.0 %copy-start.6 = (f32[16,128,128]{2,1,0:T(8,128)S(1)}, f32[16,128,128]{2,1,0:T(8,128)}, u32[]{:S(2)}) copy-start(f32[16,128,128]{2,1,0:T(8,128)} %fusion.22) | copy-start | bytes 3145732
  278.3 6.0 %copy-start.7 = (f32[16,8,128]{2,1,0:T(8,128)S(1)}, f32[16,8,128]{2,1,0:T(8,128)}, u32[]{:S(2)}) copy-start(f32[16,8,128]{2,1,0:T(8,128)} %get-tuple-element.224) | copy-start | bytes 196612
  278.3 6.0 %copy-start.8 = (f32[8]{0:T(128)S(1)}, f32[8]{0:T(128)}, u32[]{:S(2)}) copy-start(f32[8]{0:T(128)} %param.15) | copy-start | bytes 100
Sparse Core Ops, SparseCore 0:
  153.7 83.0 all-gather.3
